TPU v7x, 512 devices: a whole 4x8x8 slice. The times are simulated.
512 devices in a mesh: segment: 16 (over z, core), mp: 32 (over y, x).
Axes of the slice: x: 4, y: 8, z: 8, core: 2. Of those that a mesh axis runs over, the one named last changes fastest.
Arguments:
- rows: bfloat16 [16, 2, 128, 8192], P('segment', None, None, 'mp'), may hold values from -6 to 6
- carry: bfloat16 [16, 128, 8192], P('segment', None, 'mp'), may hold values from -6 to 6
- weights: bfloat16 [16, 2, 8192, 4096], P('segment', None, None, 'mp'), may hold values from -1.1932427 to 1.1932427
- neighbours: int32 [16, 2, 2, 2], P('segment'), may hold values from 0 to 7, all different within a row
Outputs:
- passed: bfloat16 [16, 128, 8192], P('segment', None, 'mp')
- returned: bfloat16 [16, 128, 8192], P('segment', None, 'mp')
- kv_grad: bfloat16 [1024, 2, 4096], P(None, None, 'mp')
Inputs may be any that keep to these rules, and one draw needn't show every extreme that they name: Each group's 2 neighbours are different pool blocks; pool blocks are numbered by encoder segment in order, then by row.
All inputs are finite; a program needn't handle non-finite values.
Results may differ from a plain program's by a relative error of at most 0.02.
The roundings to bfloat16 on the way count: a program that leaves them out, or rounds other values in their place, can miss the bound.
Values may be sent and summed in bfloat16 or wider, within the bound.
No kernel may reach another device: no remote copies, remote signals or barrier semaphores. Data moves between devices by JAX's collectives and lax.ppermute only.
A program may use at most 64 MiB of HBM per device.

v0:
```python
import math
import jax
import jax.numpy as jnp
from jax import lax
from jax.sharding import PartitionSpec as P

GROUP = 64
NBLEN = 128
NEIGH = 2


def from_behind(x, axis, by):
    devices = lax.axis_size(axis)
    return lax.ppermute(x, axis, [(i, (i + by) % devices) for i in range(devices)])


def attend(queries, key_rows, score_scale):
    scores = (
        jnp.einsum("cqd,ckd->cqk", queries, key_rows, preferred_element_type=jnp.float32)
        * score_scale
    )
    soft = jax.nn.softmax(scores, axis=-1)
    return (soft, soft.astype(jnp.bfloat16))


def attend_back(queries, key_rows, value_rows, soft, rounded, upstream, score_scale):
    d_soft = jnp.einsum("cqd,ckd->cqk", upstream, value_rows, preferred_element_type=jnp.float32)
    grad_values = jnp.einsum("cqk,cqd->ckd", rounded, upstream, preferred_element_type=jnp.float32)
    d_scores = soft * (d_soft - jnp.sum(d_soft * soft, axis=-1, keepdims=True))
    grad_queries = (
        jnp.einsum("cqk,ckd->cqd", d_scores, key_rows.astype(jnp.float32)) * score_scale
    ).astype(jnp.bfloat16)
    grad_keys = jnp.einsum("cqk,cqd->ckd", d_scores, queries.astype(jnp.float32)) * score_scale
    return (grad_queries, grad_keys, grad_values)


def head_sum(term, axis):
    devices = lax.axis_size(axis)
    parts = term.astype(jnp.bfloat16).reshape(devices, term.shape[0] // devices, term.shape[1])
    moved = lax.all_to_all(parts, axis, 0, 0, tiled=True)
    return jnp.sum(moved.astype(jnp.float32), axis=0).T


def segment_sum(contrib, axis):
    devices = lax.axis_size(axis)
    parts = contrib.reshape(devices, contrib.shape[0] // devices, contrib.shape[1])
    moved = lax.all_to_all(parts, axis, 0, 0, tiled=True)
    summed = jnp.sum(moved.astype(jnp.float32), axis=0).astype(jnp.bfloat16)
    spread = jnp.broadcast_to(summed[None], (devices,) + summed.shape)
    return lax.all_to_all(spread, axis, 0, 0, tiled=True).reshape(contrib.shape)


def per_device(rows, carry, weights, neighbours):
    segments = lax.axis_size("segment")
    encoders = segments // 4
    first_encoder = segments - encoders
    is_encoder = lax.axis_index("segment") >= first_encoder
    local_rows = rows[0]
    local_carry = carry[0]
    full_rows, full_carry = (
        lax.all_gather(local_rows, "mp", axis=2, tiled=True),
        lax.all_gather(local_carry, "mp", axis=1, tiled=True),
    )
    tokens = local_rows.shape[1]
    width = full_rows.shape[2]
    head = weights.shape[3]
    w_query = weights[0, 0]
    w_out = weights[0, 1]

    def encode():
        flat = full_rows.reshape(2 * tokens, width)
        keyval = jnp.concatenate(
            [
                jnp.dot(flat, w_query, preferred_element_type=jnp.float32),
                jnp.dot(flat, w_out, preferred_element_type=jnp.float32),
            ],
            axis=-1,
        ).astype(jnp.bfloat16)
        return (keyval, jnp.zeros((2 * tokens, head), jnp.bfloat16))

    def decode():
        queries = jnp.dot(
            full_rows.reshape(2 * tokens, width), w_query, preferred_element_type=jnp.float32
        ).astype(jnp.bfloat16)
        return (jnp.zeros((2 * tokens, 2 * head), jnp.bfloat16), queries)

    encoded, queries = lax.cond(is_encoder, encode, decode)
    per_encoder = 2 * tokens // NBLEN
    pool_blocks = encoders * per_encoder
    collected = lax.all_gather(encoded, "segment", axis=0, tiled=True)
    pool = collected[first_encoder * 2 * tokens :].reshape(pool_blocks, NBLEN, 2 * head)
    groups = tokens // GROUP
    local_nbr = neighbours[0]
    score_scale = 1.0 / math.sqrt(head)
    query_blocks = queries.reshape(2, groups, GROUP, head)

    def fetch(batch):
        picked = pool[local_nbr[batch]].reshape(groups, NEIGH * NBLEN, 2 * head)
        return (picked[..., :head], picked[..., head:])

    keys_fwd, values_fwd = fetch(0)
    soft_fwd, rounded_fwd = attend(query_blocks[0], keys_fwd, score_scale)
    mixed = jnp.einsum(
        "cqk,ckd->cqd", rounded_fwd, values_fwd, preferred_element_type=jnp.float32
    ).astype(jnp.bfloat16)
    mixed_flat = mixed.reshape(tokens, head)
    piece = w_out
    out_sum = head_sum(
        lax.dot_general(
            piece, mixed_flat, (((1,), (1,)), ((), ())), preferred_element_type=jnp.float32
        ),
        "mp",
    )
    forward_rows = (local_rows[0].astype(jnp.float32) + out_sum).astype(jnp.bfloat16)
    forward_rows = jnp.where(is_encoder, local_carry, forward_rows)
    passed = from_behind(forward_rows[None], "segment", 1)
    upstream = (
        jnp.dot(full_carry, w_out, preferred_element_type=jnp.float32)
        .astype(jnp.bfloat16)
        .reshape(groups, GROUP, head)
    )
    keys_back, values_back = fetch(1)
    soft_back, rounded_back = attend(query_blocks[1], keys_back, score_scale)
    grad_queries, grad_keys, grad_values = attend_back(
        query_blocks[1], keys_back, values_back, soft_back, rounded_back, upstream, score_scale
    )
    grad_flat = grad_queries.reshape(tokens, head)
    piece = w_query
    grad_input = head_sum(
        lax.dot_general(
            piece, grad_flat, (((1,), (1,)), ((), ())), preferred_element_type=jnp.float32
        ),
        "mp",
    )
    back = local_carry.astype(jnp.float32) + grad_input
    back_rows = jnp.where(is_encoder, local_carry, back.astype(jnp.bfloat16))
    returned = from_behind(back_rows[None], "segment", -1)
    onehot = (
        local_nbr[1][..., None] == jnp.arange(pool_blocks, dtype=jnp.int32)[None, None, :]
    ).astype(jnp.float32)
    grad_keyval = jnp.concatenate([grad_keys, grad_values], axis=-1).reshape(
        groups, NEIGH, NBLEN, 2 * head
    )
    contrib = jnp.einsum("cbp,cbrf->prf", onehot, grad_keyval)
    contrib = jnp.where(is_encoder, jnp.zeros_like(contrib), contrib)
    pooled = segment_sum(
        contrib.astype(jnp.bfloat16).reshape(pool_blocks * NBLEN, 2 * head), "segment"
    )
    kv_grad = pooled.reshape(pool_blocks * NBLEN, 2, head)
    return (passed, returned, kv_grad)


def solution(mesh):
    placed = (
        P("segment", None, None, "mp"),
        P("segment", None, "mp"),
        P("segment", None, None, "mp"),
        P("segment", None, None, None),
    )
    return jax.shard_map(
        per_device,
        mesh=mesh,
        in_specs=placed,
        out_specs=(P("segment", None, "mp"), P("segment", None, "mp"), P(None, None, "mp")),
        check_vma=False,
    )
```

profile of v0, /device:TPU:1, one launch (start us, length us, event | category | flops | bytes accessed | tf_op | source)
XLA Modules:
  0.0 407.9 jit_solution(1906226420023038693)
XLA Ops:
  7.2 0.7 all-gather.8.cloned.1.call-update
  7.9 0.7 all-gather.10.cloned.1.call-update
  8.7 3.8 slice_bitcast_fusion
  12.5 89.2 %all-gather.8.cloned.1.call-done = bf16[1,2,128,8192]{3,2,1,0:T(8,128)(2,1)} async-done(((bf16[1,2,128,256]{3,2,1,0:T(8,128)(2,1)}), bf16[1,2,128,8192]{3,2,1,0:T(8,128)(2,1)}) %all-gather.8.cloned.1.call-update) | async-done | bytes 4194320 | tf_op jit(solution)/shard_map/all_gather | solution.py:61
  101.8 3.5 conditional.1
  101.8 3.4 convolution_convert_fusion
  105.3 0.6 copy-done.1
  106.2 79.5 %all-gather.10.cloned.1.call-done = bf16[1,128,8192]{2,1,0:T(8,128)(2,1)} async-done(((bf16[1,128,256]{2,1,0:T(8,128)(2,1)}), bf16[1,128,8192]{2,1,0:T(8,128)(2,1)}) %all-gather.10.cloned.1.call-update) | async-done | bytes 2097168 | tf_op jit(solution)/shard_map/all_gather | solution.py:62
  185.7 2.9 fusion.11
  188.6 45.9 %all-gather.6.cloned.1.call-done = bf16[4096,256]{1,0:T(8,128)(2,1)} async-done(((bf16[256,256]{1,0:T(8,128)(2,1)}), bf16[4096,256]{1,0:T(8,128)(2,1)}) %all-gather.6.cloned.1.call-update) | async-done | bytes 2097168 | tf_op jit(solution)/shard_map/all_gather | solution.py:90
  234.5 1.1 slice.67
  235.6 0.6 gather_fusion.1
  238.8 0.9 copy.19
  239.7 4.4 %all-to-all-start.2 = ((bf16[16,64,256]{2,1,0:T(8,128)(2,1)}), bf16[16,64,256]{2,1,0:T(8,128)(2,1)S(1)}, u32[]{:S(2)}, u32[]{:S(2)}) async-start(bf16[16,64,256]{2,1,0:T(8,128)(2,1)} %bitcast.28), calls=%async_computation.2 | async-start | bytes 1048576 | tf_op jit(solution)/shard_map/all_to_all | solution.py:47
  244.5 2.3 convolution_convert_fusion.3
  246.8 1.6 copy.25
  248.4 13.1 %all-to-all-done.2 = bf16[16,64,256]{2,1,0:T(8,128)(2,1)S(1)} async-done(((bf16[16,64,256]{2,1,0:T(8,128)(2,1)}), bf16[16,64,256]{2,1,0:T(8,128)(2,1)S(1)}, u32[]{:S(2)}, u32[]{:S(2)}) %all-to-all-start.2) | async-done | bytes 524320 | tf_op jit(solution)/shard_map/all_to_all | solution.py:47
  261.5 9.3 %all-to-all-start.1 = ((bf16[32,256,128]{1,2,0:T(8,128)(2,1)}), bf16[32,256,128]{1,2,0:T(8,128)(2,1)S(1)}, u32[]{:S(2)}, u32[]{:S(2)}) async-start(bf16[32,256,128]{1,2,0:T(8,128)(2,1)} %bitcast.105), calls=%async_computation.1 | async-start | bytes 4194304 | tf_op jit(solution)/shard_map/all_to_all | solution.py:40
  270.8 0.6 gather_fusion
  272.1 2.3 convolution_convert_fusion.4
  274.4 1.6 copy.26
  276.0 45.4 %all-to-all-done.1 = bf16[32,256,128]{1,2,0:T(8,128)(2,1)S(1)} async-done(((bf16[32,256,128]{1,2,0:T(8,128)(2,1)}), bf16[32,256,128]{1,2,0:T(8,128)(2,1)S(1)}, u32[]{:S(2)}, u32[]{:S(2)}) %all-to-all-start.1) | async-done | bytes 2097184 | tf_op jit(solution)/shard_map/all_to_all | solution.py:40
  321.4 5.1 %all-to-all-start = ((bf16[32,256,128]{1,2,0:T(8,128)(2,1)}), bf16[32,256,128]{1,2,0:T(8,128)(2,1)}, u32[]{:S(2)}, u32[]{:S(2)}) async-start(bf16[32,256,128]{1,2,0:T(8,128)(2,1)} %bitcast.106), calls=%async_computation | async-start | bytes 4194304 | tf_op jit(solution)/shard_map/all_to_all | solution.py:40
  326.7 48.3 %all-to-all-done = bf16[32,256,128]{1,2,0:T(8,128)(2,1)} async-done(((bf16[32,256,128]{1,2,0:T(8,128)(2,1)}), bf16[32,256,128]{1,2,0:T(8,128)(2,1)}, u32[]{:S(2)}, u32[]{:S(2)}) %all-to-all-start) | async-done | bytes 2097184 | tf_op jit(solution)/shard_map/all_to_all | solution.py:40
  375.0 0.8 broadcast_in_dim.11
  375.9 6.0 %all-to-all-start.3 = ((bf16[16,64,256]{2,1,0:T(8,128)(2,1)}), bf16[16,64,256]{2,1,0:T(8,128)(2,1)S(1)}, u32[]{:S(2)}, u32[]{:S(2)}) async-start(bf16[16,64,256]{2,1,0:T(8,128)(2,1)} %broadcast_in_dim.11), calls=%async_computation.3 | async-start | bytes 1048576 | tf_op jit(solution)/shard_map/all_to_all | solution.py:50
  382.2 1.9 convert_reduce_fusion.1
  384.1 1.7 collective-permute-start
  385.8 13.4 %all-to-all-done.3 = bf16[16,64,256]{2,1,0:T(8,128)(2,1)S(1)} async-done(((bf16[16,64,256]{2,1,0:T(8,128)(2,1)}), bf16[16,64,256]{2,1,0:T(8,128)(2,1)S(1)}, u32[]{:S(2)}, u32[]{:S(2)}) %all-to-all-start.3) | async-done | bytes 524320 | tf_op jit(solution)/shard_map/all_to_all | solution.py:50
  399.2 0.9 reshape_reshape.7
  400.2 0.6 copy.35
  400.8 0.6 copy.36
  (39 shorter events, 4.5 us)
Async XLA Ops:
  7.2 94.6 %all-gather.8.cloned.1.call-start = ((), (), s32[]{:S(2)}) async-start(), calls=%async_computation.5 | async-start | bytes 4325376 | tf_op jit(solution)/shard_map/all_gather | solution.py:61
  7.9 177.8 %all-gather.10.cloned.1.call-start = ((), (), s32[]{:S(2)}) async-start(), calls=%async_computation.6 | async-start | bytes 2162688 | tf_op jit(solution)/shard_map/all_gather | solution.py:62
  8.6 225.9 %all-gather.6.cloned.1.call-start = ((), (), s32[]{:S(2)}) async-start(), calls=%async_computation.4 | async-start | bytes 2228224 | tf_op jit(solution)/shard_map/all_gather | solution.py:90
  101.8 4.2 %copy-start.4 = (s32[1,2,2,2]{3,2,1,0:T(2,128)S(1)}, s32[1,2,2,2]{3,2,1,0:T(2,128)}, u32[]{:S(2)}) copy-start(s32[1,2,2,2]{3,2,1,0:T(2,128)} %param.9) | copy-start | bytes 100
  105.3 0.7 copy-start.1
  239.7 21.7 %all-to-all-start.2 = ((bf16[16,64,256]{2,1,0:T(8,128)(2,1)}), bf16[16,64,256]{2,1,0:T(8,128)(2,1)S(1)}, u32[]{:S(2)}, u32[]{:S(2)}) async-start(bf16[16,64,256]{2,1,0:T(8,128)(2,1)} %bitcast.28), calls=%async_computation.2 | async-start | bytes 1048576 | tf_op jit(solution)/shard_map/all_to_all | solution.py:47
  261.5 60.0 %all-to-all-start.1 = ((bf16[32,256,128]{1,2,0:T(8,128)(2,1)}), bf16[32,256,128]{1,2,0:T(8,128)(2,1)S(1)}, u32[]{:S(2)}, u32[]{:S(2)}) async-start(bf16[32,256,128]{1,2,0:T(8,128)(2,1)} %bitcast.105), calls=%async_computation.1 | async-start | bytes 4194304 | tf_op jit(solution)/shard_map/all_to_all | solution.py:40
  321.4 53.6 %all-to-all-start = ((bf16[32,256,128]{1,2,0:T(8,128)(2,1)}), bf16[32,256,128]{1,2,0:T(8,128)(2,1)}, u32[]{:S(2)}, u32[]{:S(2)}) async-start(bf16[32,256,128]{1,2,0:T(8,128)(2,1)} %bitcast.106), calls=%async_computation | async-start | bytes 4194304 | tf_op jit(solution)/shard_map/all_to_all | solution.py:40
  375.9 23.4 %all-to-all-start.3 = ((bf16[16,64,256]{2,1,0:T(8,128)(2,1)}), bf16[16,64,256]{2,1,0:T(8,128)(2,1)S(1)}, u32[]{:S(2)}, u32[]{:S(2)}) async-start(bf16[16,64,256]{2,1,0:T(8,128)(2,1)} %broadcast_in_dim.11), calls=%async_computation.3 | async-start | bytes 1048576 | tf_op jit(solution)/shard_map/all_to_all | solution.py:50
  381.9 2.2 copy-start.2
  381.9 2.2 copy-start.3
  384.1 16.0 %collective-permute-start = (bf16[1,128,256]{2,1,0:T(8,128)(2,1)S(1)}, bf16[1,128,256]{2,1,0:T(8,128)(2,1)S(1)}, u32[]{:S(2)}, u32[]{:S(2)}) collective-permute-start(bf16[1,128,256]{2,1,0:T(8,128)(2,1)S(1)} %get-tuple-element.53), channel_id=1, source_target_pairs={{0,32},{32,64},{64,96},{96,128},{128,160},{160,192},{192,224},{224... | collective-permute-start | bytes 196616 | tf_op jit(solution)/shard_map/ppermute | solution.py:14
  385.8 14.4 %collective-permute-start.1 = (bf16[1,128,256]{2,1,0:T(8,128)(2,1)S(1)}, bf16[1,128,256]{2,1,0:T(8,128)(2,1)S(1)}, u32[]{:S(2)}, u32[]{:S(2)}) collective-permute-start(bf16[1,128,256]{2,1,0:T(8,128)(2,1)S(1)} %get-tuple-element.52), channel_id=1, source_target_pairs={{0,480},{32,0},{64,32},{96,64},{128,96},{160,128},{192,160},{224,1... | collective-permute-start | bytes 196616 | tf_op jit(solution)/shard_map/ppermute | solution.py:14
Sparse Core Ops, SparseCore 0:
  11.0 90.6 all-gather.7
  104.8 80.8 all-gather.9
  188.4 46.0 all-gather.5
where the time goes:
time: 409 us; the launch traced here: 408 us
  waiting for transfers between devices  336 us (82%)
  starting transfers between devices  26.6 us (7%)
  local copies, waits for them, and re-layouts  14.6 us (4%)
  between operations  14 us (3%)
  matrix products  13.5 us (3%)
    all_to_all x2, waiting for transfers between devices, head_sum(): moved = lax.all_to_all(parts, axis, 0, 0, tiled=True)  93.8 us
    all_gather x1, waiting for transfers between devices, per_device(): lax.all_gather(local_rows, 'mp', axis=2, tiled=True)  89.2 us
    all_gather x1, waiting for transfers between devices, per_device(): lax.all_gather(local_carry, 'mp', axis=1, tiled=True)  79.5 us
    all_gather x1, waiting for transfers between devices, per_device(): collected = lax.all_gather(encoded, 'segment', axis=0, tiled=True)  45.9 us
    all_to_all x2, starting transfers between devices, head_sum(): moved = lax.all_to_all(parts, axis, 0, 0, tiled=True)  14.4 us
    all_to_all x1, waiting for transfers between devices, segment_sum(): return lax.all_to_all(spread, axis, 0, 0, tiled=True).reshape(contrib.shape)  13.4 us
    all_to_all x1, waiting for transfers between devices, segment_sum(): moved = lax.all_to_all(parts, axis, 0, 0, tiled=True)  13.1 us
  transfers between devices with their start and end apart: 9, of which 7 were waited for; matrix products, arithmetic and copies ran while one was open for 6% of the time, Pallas kernels for 0%

commit v1 on v0

--- a/solution.py
+++ b/solution.py
@@ -58,7 +58,9 @@
     local_rows = rows[0]
     local_carry = carry[0]
     full_rows, full_carry = (
-        lax.all_gather(local_rows, "mp", axis=2, tiled=True),
+        jnp.concatenate(
+            lax.all_to_all(jnp.stack([local_rows] * lax.axis_size("mp")), "mp", 0, 0), axis=2
+        ),
         lax.all_gather(local_carry, "mp", axis=1, tiled=True),
     )
     tokens = local_rows.shape[1]

time: 409 us -> 361 us (0.88)
  waiting for transfers between devices: 336 us -> 268 us
  local copies, waits for them, and re-layouts: 14.6 us -> 26.8 us
  starting transfers between devices: 26.6 us -> 37.2 us
    all_to_all x0 -> x1, waiting for transfers between devices: none -> 91.8 us  [per_device(): lax.all_to_all(jnp.stack([local_rows] * lax.axis_size('mp')), 'mp', 0, 0)]
    all_gather x1 -> x0, waiting for transfers between devices: 89.2 us -> none  [per_device(): lax.all_gather(local_rows, 'mp', axis=2, tiled=True)]
    all_gather x1, waiting for transfers between devices: 79.5 us -> 6.43 us  [per_device(): lax.all_gather(local_carry, 'mp', axis=1, tiled=True)]
    all_to_all x0 -> x1, starting transfers between devices: none -> 10.6 us  [per_device(): lax.all_to_all(jnp.stack([local_rows] * lax.axis_size('mp')), 'mp', 0, 0)]
    another operation x1 -> x3, local copies, waits for them, and re-layouts: 0.01 us -> 7.98 us
    cond x0 -> x1, local copies, waits for them, and re-layouts: none -> 4.29 us
  transfers between devices with their start and end apart: 9 -> 9, of which waited for: 7 -> 7; matrix products, arithmetic and copies ran while one was open for 6% -> 8% of each run, Pallas kernels for 0% -> 0%
where the time goes in v1:
time: 361 us; the launch traced here: 360 us
  waiting for transfers between devices  268 us (74%)
  starting transfers between devices  37.2 us (10%)
  local copies, waits for them, and re-layouts  26.8 us (7%)
  between operations  14.3 us (4%)
  matrix products  11.3 us (3%)
    all_to_all x2, waiting for transfers between devices, head_sum(): moved = lax.all_to_all(parts, axis, 0, 0, tiled=True)  93.8 us
    all_to_all x1, waiting for transfers between devices, per_device(): lax.all_to_all(jnp.stack([local_rows] * lax.axis_size('mp')), 'mp', 0, 0)  91.8 us
    all_gather x1, waiting for transfers between devices, per_device(): collected = lax.all_gather(encoded, 'segment', axis=0, tiled=True)  48.4 us
    all_to_all x2, starting transfers between devices, head_sum(): moved = lax.all_to_all(parts, axis, 0, 0, tiled=True)  14.4 us
    all_to_all x1, waiting for transfers between devices, segment_sum(): return lax.all_to_all(spread, axis, 0, 0, tiled=True).reshape(contrib.shape)  13.4 us
    all_to_all x1, waiting for transfers between devices, segment_sum(): moved = lax.all_to_all(parts, axis, 0, 0, tiled=True)  13.1 us
    all_to_all x1, starting transfers between devices, per_device(): lax.all_to_all(jnp.stack([local_rows] * lax.axis_size('mp')), 'mp', 0, 0)  10.6 us
  transfers between devices with their start and end apart: 9, of which 7 were waited for; matrix products, arithmetic and copies ran while one was open for 8% of the time, Pallas kernels for 0%

profile of v1, /device:TPU:1, one launch (start us, length us, event | category | flops | bytes accessed | tf_op | source)
XLA Modules:
  0.0 360.4 jit_solution(15083149262808522817)
XLA Ops:
  7.2 3.4 stack.3
  10.5 10.6 %all-to-all-start = ((bf16[32,2,128,256]{3,2,1,0:T(8,128)(2,1)}), bf16[32,2,128,256]{3,2,1,0:T(8,128)(2,1)}, u32[]{:S(2)}, u32[]{:S(2)}) async-start(bf16[32,2,128,256]{3,2,1,0:T(8,128)(2,1)} %stack.3), calls=%async_computation | async-start | bytes 8388608 | tf_op jit(solution)/shard_map/all_to_all | solution.py:62
  21.2 0.7 all-gather.6.cloned.1.call-update
  22.0 3.8 %slice_bitcast_fusion = (bf16[8192,128]{1,0:T(8,128)(2,1)}, bf16[8192,128]{1,0:T(8,128)(2,1)S(1)}) fusion(bf16[1,2,8192,128]{3,2,1,0:T(8,128)(2,1)} %param.8), kind=kLoop, calls=%fused_computation.16 | loop fusion | bytes 8388608 | tf_op jit(solution)/shard_map/squeeze | solution.py:70
  25.8 91.8 %all-to-all-done = bf16[32,2,128,256]{3,2,1,0:T(8,128)(2,1)} async-done(((bf16[32,2,128,256]{3,2,1,0:T(8,128)(2,1)}), bf16[32,2,128,256]{3,2,1,0:T(8,128)(2,1)}, u32[]{:S(2)}, u32[]{:S(2)}) %all-to-all-start) | async-done | bytes 4194336 | tf_op jit(solution)/shard_map/all_to_all | solution.py:62
  117.6 10.4 %conditional.1 = (bf16[256,256]{1,0:T(8,128)(2,1)S(1)}, bf16[2,64,128]{2,1,0:T(8,128)(2,1)S(1)}, bf16[2,64,128]{2,1,0:T(8,128)(2,1)S(1)}) conditional(s32[]{:T(128)} %convert_element_type.67, (bf16[2,128,32,256]{3,1,0,2:T(8,128)(2,1)}, bf16[8192,128]{1,0:T(8,128)(2,1)S(1)}) %tuple.22, (bf16[2,128,32,256]{3,1,0,2:T(8,128)(2,1)}, ...), branch_computations={%region_0.0_spmd, %region_1.0_spmd} | conditional | flops 1074069504 | bytes 38469688 | solution.py:89
  117.6 4.6 %copy.15 = bf16[2,128,32,256]{3,2,1,0:T(8,128)(2,1)S(1)} copy(bf16[2,128,32,256]{3,1,0,2:T(8,128)(2,1)} %get-tuple-element.48) | data formatting | bytes 8388608 | tf_op jit(solution)/shard_map
  122.2 4.3 %copy.23 = bf16[32,8,32,256]{3,1,2,0:T(8,128)(2,1)S(1)} copy(bf16[32,8,32,256]{3,2,1,0:T(8,128)(2,1)S(1)} %bitcast.108) | data formatting | bytes 8388608 | tf_op jit(solution)/shard_map/cond
  126.5 1.3 convolution_convert_fusion
  128.0 0.6 copy-done.1
  128.9 6.4 %all-gather.6.cloned.1.call-done = bf16[1,128,8192]{2,1,0:T(8,128)(2,1)} async-done(((bf16[1,128,256]{2,1,0:T(8,128)(2,1)}), bf16[1,128,8192]{2,1,0:T(8,128)(2,1)}) %all-gather.6.cloned.1.call-update) | async-done | bytes 2097168 | tf_op jit(solution)/shard_map/all_gather | solution.py:64
  135.3 2.9 fusion.11
  138.2 48.4 %all-gather.4.cloned.1.call-done = bf16[4096,256]{1,0:T(8,128)(2,1)} async-done(((bf16[256,256]{1,0:T(8,128)(2,1)}), bf16[4096,256]{1,0:T(8,128)(2,1)}) %all-gather.4.cloned.1.call-update) | async-done | bytes 2097168 | tf_op jit(solution)/shard_map/all_gather | solution.py:92
  186.6 1.1 slice.67
  190.9 0.9 copy.21
  191.8 4.4 %all-to-all-start.3 = ((bf16[16,64,256]{2,1,0:T(8,128)(2,1)}), bf16[16,64,256]{2,1,0:T(8,128)(2,1)S(1)}, u32[]{:S(2)}, u32[]{:S(2)}) async-start(bf16[16,64,256]{2,1,0:T(8,128)(2,1)} %bitcast.27), calls=%async_computation.3 | async-start | bytes 1048576 | tf_op jit(solution)/shard_map/all_to_all | solution.py:47
  196.6 2.3 convolution_convert_fusion.3
  198.9 1.6 copy.29
  200.5 13.1 %all-to-all-done.3 = bf16[16,64,256]{2,1,0:T(8,128)(2,1)S(1)} async-done(((bf16[16,64,256]{2,1,0:T(8,128)(2,1)}), bf16[16,64,256]{2,1,0:T(8,128)(2,1)S(1)}, u32[]{:S(2)}, u32[]{:S(2)}) %all-to-all-start.3) | async-done | bytes 524320 | tf_op jit(solution)/shard_map/all_to_all | solution.py:47
  213.6 9.3 %all-to-all-start.2 = ((bf16[32,256,128]{1,2,0:T(8,128)(2,1)}), bf16[32,256,128]{1,2,0:T(8,128)(2,1)S(1)}, u32[]{:S(2)}, u32[]{:S(2)}) async-start(bf16[32,256,128]{1,2,0:T(8,128)(2,1)} %bitcast.110), calls=%async_computation.2 | async-start | bytes 4194304 | tf_op jit(solution)/shard_map/all_to_all | solution.py:40
  224.2 2.3 convolution_convert_fusion.4
  226.5 1.6 copy.30
  228.1 45.4 %all-to-all-done.2 = bf16[32,256,128]{1,2,0:T(8,128)(2,1)S(1)} async-done(((bf16[32,256,128]{1,2,0:T(8,128)(2,1)}), bf16[32,256,128]{1,2,0:T(8,128)(2,1)S(1)}, u32[]{:S(2)}, u32[]{:S(2)}) %all-to-all-start.2) | async-done | bytes 2097184 | tf_op jit(solution)/shard_map/all_to_all | solution.py:40
  273.5 5.1 %all-to-all-start.1 = ((bf16[32,256,128]{1,2,0:T(8,128)(2,1)}), bf16[32,256,128]{1,2,0:T(8,128)(2,1)}, u32[]{:S(2)}, u32[]{:S(2)}) async-start(bf16[32,256,128]{1,2,0:T(8,128)(2,1)} %bitcast.111), calls=%async_computation.1 | async-start | bytes 4194304 | tf_op jit(solution)/shard_map/all_to_all | solution.py:40
  278.8 48.3 %all-to-all-done.1 = bf16[32,256,128]{1,2,0:T(8,128)(2,1)} async-done(((bf16[32,256,128]{1,2,0:T(8,128)(2,1)}), bf16[32,256,128]{1,2,0:T(8,128)(2,1)}, u32[]{:S(2)}, u32[]{:S(2)}) %all-to-all-start.1) | async-done | bytes 2097184 | tf_op jit(solution)/shard_map/all_to_all | solution.py:40
  327.1 0.8 broadcast_in_dim.11
  328.0 6.0 %all-to-all-start.4 = ((bf16[16,64,256]{2,1,0:T(8,128)(2,1)}), bf16[16,64,256]{2,1,0:T(8,128)(2,1)S(1)}, u32[]{:S(2)}, u32[]{:S(2)}) async-start(bf16[16,64,256]{2,1,0:T(8,128)(2,1)} %broadcast_in_dim.11), calls=%async_computation.4 | async-start | bytes 1048576 | tf_op jit(solution)/shard_map/all_to_all | solution.py:50
  334.3 1.9 convert_reduce_fusion.1
  336.3 1.7 collective-permute-start
  337.9 13.4 %all-to-all-done.4 = bf16[16,64,256]{2,1,0:T(8,128)(2,1)S(1)} async-done(((bf16[16,64,256]{2,1,0:T(8,128)(2,1)}), bf16[16,64,256]{2,1,0:T(8,128)(2,1)S(1)}, u32[]{:S(2)}, u32[]{:S(2)}) %all-to-all-start.4) | async-done | bytes 524320 | tf_op jit(solution)/shard_map/all_to_all | solution.py:50
  351.4 0.9 reshape_reshape.15
  352.3 0.6 copy.39
  (41 shorter events, 6.2 us)
Async XLA Ops:
  10.5 107.0 %all-to-all-start = ((bf16[32,2,128,256]{3,2,1,0:T(8,128)(2,1)}), bf16[32,2,128,256]{3,2,1,0:T(8,128)(2,1)}, u32[]{:S(2)}, u32[]{:S(2)}) async-start(bf16[32,2,128,256]{3,2,1,0:T(8,128)(2,1)} %stack.3), calls=%async_computation | async-start | bytes 8388608 | tf_op jit(solution)/shard_map/all_to_all | solution.py:62
  21.2 114.1 %all-gather.6.cloned.1.call-start = ((), (), s32[]{:S(2)}) async-start(), calls=%async_computation.6 | async-start | bytes 2162688 | tf_op jit(solution)/shard_map/all_gather | solution.py:64
  21.9 164.7 %all-gather.4.cloned.1.call-start = ((), (), s32[]{:S(2)}) async-start(), calls=%async_computation.5 | async-start | bytes 2228224 | tf_op jit(solution)/shard_map/all_gather | solution.py:92
  117.6 11.1 %copy-start.4 = (s32[1,2,2,2]{3,2,1,0:T(2,128)S(1)}, s32[1,2,2,2]{3,2,1,0:T(2,128)}, u32[]{:S(2)}) copy-start(s32[1,2,2,2]{3,2,1,0:T(2,128)} %param.9) | copy-start | bytes 100
  128.0 0.7 copy-start.1
  191.8 21.7 %all-to-all-start.3 = ((bf16[16,64,256]{2,1,0:T(8,128)(2,1)}), bf16[16,64,256]{2,1,0:T(8,128)(2,1)S(1)}, u32[]{:S(2)}, u32[]{:S(2)}) async-start(bf16[16,64,256]{2,1,0:T(8,128)(2,1)} %bitcast.27), calls=%async_computation.3 | async-start | bytes 1048576 | tf_op jit(solution)/shard_map/all_to_all | solution.py:47
  213.6 60.0 %all-to-all-start.2 = ((bf16[32,256,128]{1,2,0:T(8,128)(2,1)}), bf16[32,256,128]{1,2,0:T(8,128)(2,1)S(1)}, u32[]{:S(2)}, u32[]{:S(2)}) async-start(bf16[32,256,128]{1,2,0:T(8,128)(2,1)} %bitcast.110), calls=%async_computation.2 | async-start | bytes 4194304 | tf_op jit(solution)/shard_map/all_to_all | solution.py:40
  273.5 53.6 %all-to-all-start.1 = ((bf16[32,256,128]{1,2,0:T(8,128)(2,1)}), bf16[32,256,128]{1,2,0:T(8,128)(2,1)}, u32[]{:S(2)}, u32[]{:S(2)}) async-start(bf16[32,256,128]{1,2,0:T(8,128)(2,1)} %bitcast.111), calls=%async_computation.1 | async-start | bytes 4194304 | tf_op jit(solution)/shard_map/all_to_all | solution.py:40
  328.0 23.4 %all-to-all-start.4 = ((bf16[16,64,256]{2,1,0:T(8,128)(2,1)}), bf16[16,64,256]{2,1,0:T(8,128)(2,1)S(1)}, u32[]{:S(2)}, u32[]{:S(2)}) async-start(bf16[16,64,256]{2,1,0:T(8,128)(2,1)} %broadcast_in_dim.11), calls=%async_computation.4 | async-start | bytes 1048576 | tf_op jit(solution)/shard_map/all_to_all | solution.py:50
  334.0 2.2 copy-start.2
  334.0 2.2 copy-start.3
  336.3 16.0 %collective-permute-start = (bf16[1,128,256]{2,1,0:T(8,128)(2,1)S(1)}, bf16[1,128,256]{2,1,0:T(8,128)(2,1)S(1)}, u32[]{:S(2)}, u32[]{:S(2)}) collective-permute-start(bf16[1,128,256]{2,1,0:T(8,128)(2,1)S(1)} %get-tuple-element.58), channel_id=1, source_target_pairs={{0,32},{32,64},{64,96},{96,128},{128,160},{160,192},{192,224},{224... | collective-permute-start | bytes 196616 | tf_op jit(solution)/shard_map/ppermute | solution.py:14
  337.9 14.4 %collective-permute-start.1 = (bf16[1,128,256]{2,1,0:T(8,128)(2,1)S(1)}, bf16[1,128,256]{2,1,0:T(8,128)(2,1)S(1)}, u32[]{:S(2)}, u32[]{:S(2)}) collective-permute-start(bf16[1,128,256]{2,1,0:T(8,128)(2,1)S(1)} %get-tuple-element.57), channel_id=1, source_target_pairs={{0,480},{32,0},{64,32},{96,64},{128,96},{160,128},{192,160},{224,1... | collective-permute-start | bytes 196616 | tf_op jit(solution)/shard_map/ppermute | solution.py:14
Sparse Core Ops, SparseCore 0:
  25.1 110.1 all-gather.5
  138.0 48.6 all-gather.3
